TPU v7x, 128 devices: a whole 4x4x4 slice. The times are simulated.
128 devices in a mesh: chan: 32 (over z, y_lo, x), freq: 4 (over y_hi, core).
Axes of the slice: x: 4, y: 4 (y_hi: 2, y_lo: 2; y = y_hi * 2 + y_lo), z: 4, core: 2. Of those that a mesh axis runs over, the one named last changes fastest.
Arguments:
- strain: bfloat16 [2048, 256, 1024], P('chan', 'freq'), may hold values from -6 to 6
- mad_index: int32 [2048], P('chan'), may hold values from 0 to 15
- mad_table: float32 [16], replicated, may hold values from 0.25 to 2.5
- freq_bins: int32 [64], replicated, may hold values from 1 to 511
- valid_count: int32 [2048], P('chan'), may hold values from 64 to 256
Outputs:
- cross: float32 [64, 2, 2048, 2048], P('freq', None, 'chan')
All inputs are finite; a program needn't handle non-finite values.
Results may differ from a plain program's by a relative error of at most 0.0057.
Values may be sent and summed in bfloat16 or wider, within the bound.
No kernel may reach another device: no remote copies, remote signals or barrier semaphores. Data moves between devices by JAX's collectives and lax.ppermute only.
A program may use at most 256 MiB of HBM per device.

v0:
```python
import math

import jax
import jax.numpy as jnp
from jax import lax
from jax.sharding import PartitionSpec as P

CLIP_FACTOR = 2.0


def passed_along(block, axis, distance):
    devices = range(lax.axis_size(axis))
    route = [((i - distance) % len(devices), i) for i in devices]
    return lax.ppermute(block, axis, route)


def dft_table(freq_bins, length):
    samples = jnp.arange(length, dtype=jnp.int32)
    phase_index = samples[:, None] * freq_bins[None, :] % length
    angle = phase_index.astype(jnp.float32) * (2.0 * math.pi / length)
    taper = 0.5 - 0.5 * jnp.cos(samples.astype(jnp.float32) * (2.0 * math.pi / length))
    cosine = taper[:, None] * jnp.cos(angle)
    sine = -taper[:, None] * jnp.sin(angle)
    stacked = jnp.stack([cosine, sine], axis=2)
    return stacked.reshape(length, 2 * freq_bins.shape[0]).astype(jnp.bfloat16)


def clip_scales(mad_index, mad_table):
    entries = jnp.arange(mad_table.shape[0], dtype=jnp.int32)
    matches = mad_index[:, None] == entries[None, :]
    return jnp.sum(jnp.where(matches, mad_table[None, :], 0.0), axis=1)


def cross_block(own_panel, visitor):
    bin_count, _, row_count, win_count = own_panel.shape
    col_count = visitor.shape[2]
    products = jnp.einsum(
        "fcw,fdw->fcd",
        own_panel.reshape(bin_count, 2 * row_count, win_count),
        visitor.reshape(bin_count, 2 * col_count, win_count),
        preferred_element_type=jnp.float32,
    )
    products = products.reshape(bin_count, 2, row_count, 2, col_count)
    real_part = products[:, 0, :, 0] + products[:, 1, :, 1]
    imag_part = products[:, 1, :, 0] - products[:, 0, :, 1]
    return jnp.stack([real_part, imag_part], axis=1)


def place_block(result, block, column_first):
    return lax.dynamic_update_slice(result, block, (0, 0, 0, column_first))


def per_device(strain, mad_index, mad_table, freq_bins, valid_count):
    channels, win_local, length = strain.shape
    bin_count = freq_bins.shape[0]
    limits = (clip_scales(mad_index, mad_table) * CLIP_FACTOR)[:, None, None]
    clipped = jnp.clip(strain.astype(jnp.float32), -limits, limits).astype(jnp.bfloat16)
    table = dft_table(freq_bins, length)
    flat_rows = clipped.reshape(channels * win_local, length)
    spectrum = lax.dot_general(
        table, flat_rows, (((0,), (1,)), ((), ())), preferred_element_type=jnp.float32
    )
    window_ids = lax.axis_index("freq") * win_local + jnp.arange(win_local, dtype=jnp.int32)
    counts = valid_count.astype(jnp.float32)
    weights = jnp.where(
        window_ids[None, :] < valid_count[:, None], 1.0 / jnp.sqrt(counts)[:, None], 0.0
    )
    weighted = (spectrum * weights.reshape(1, channels * win_local)).astype(jnp.bfloat16)
    weighted = weighted.reshape(bin_count, 2, channels, win_local)
    panels = lax.all_to_all(weighted, "freq", split_axis=0, concat_axis=3, tiled=True)
    cycle_size = lax.axis_size("chan")
    my_index = lax.axis_index("chan")
    bin_local = panels.shape[0]
    output = jnp.zeros((bin_local, 2, channels, cycle_size * channels), jnp.float32)
    output = place_block(output, cross_block(panels, panels), my_index * channels)

    def step_one(step_idx, carry):
        visitor, result = carry
        visitor = passed_along(visitor, "chan", 1)
        source = (my_index - step_idx) % cycle_size
        return (visitor, place_block(result, cross_block(panels, visitor), source * channels))

    _, output = lax.fori_loop(1, cycle_size, step_one, (panels, output))
    return output


def solution(mesh):
    return jax.shard_map(
        per_device,
        mesh=mesh,
        in_specs=(P("chan", "freq", None), P("chan"), P(), P(), P("chan")),
        out_specs=P("freq", None, "chan", None),
        check_vma=False,
    )
```

profile of v0, /device:TPU:0, one launch (start us, length us, event | category | flops | bytes accessed | tf_op | source)
XLA Modules:
  0.0 1242.9 jit_solution(13142907858406404678)
XLA Ops:
  4.6 10.8 minimum_convert_fusion
  31.2 16.0 %all-to-all-done = bf16[4,2,65536]{2,1,0:T(2,128)(2,1)S(1)} async-done(((bf16[4,2,65536]{2,1,0:T(2,128)(2,1)}), bf16[4,2,65536]{2,1,0:T(2,128)(2,1)S(1)}, u32[]{:S(2)}, u32[]{:S(2)}) %all-to-all-start) | async-done | bytes 1048608 | tf_op jit(solution)/shard_map/all_to_all | solution.py:70
  78.3 1152.7 %while.17 = (s32[]{:T(128)}, bf16[16,2,64,256]{3,2,1,0:T(8,128)(2,1)S(1)}, f32[16,2,64,2048]{3,2,0,1:T(8,128)}, bf16[16,2,64,256]{3,2,1,0:T(8,128)(2,1)}, s32[]{...) while((s32[]{:T(128)}, ...), condition=%wide.region_2.3_spmd, body=%wide.region_1.2_spmd.sunk | while | flops 134479872 | bytes 25690480 | solution.py:83
  82.7 27.3 %collective-permute-done = bf16[16,2,64,256]{3,2,1,0:T(8,128)(2,1)S(1)} collective-permute-done((bf16[16,2,64,256]{3,2,1,0:T(8,128)(2,1)S(1)}, bf16[16,2,64,256]{3,2,1,0:T(8,128)(2,1)S(1)}, u32[]{:S(2)}, u32[]{:S(2)}) %collective-permute-start) | collective-permute-done | bytes 1048608 | tf_op jit(solution)/shard_map/while/body/eval_jaxpr/ppermute | solution.py:14
  124.8 28.3 %collective-permute-done = bf16[16,2,64,256]{3,2,1,0:T(8,128)(2,1)S(1)} collective-permute-done((bf16[16,2,64,256]{3,2,1,0:T(8,128)(2,1)S(1)}, bf16[16,2,64,256]{3,2,1,0:T(8,128)(2,1)S(1)}, u32[]{:S(2)}, u32[]{:S(2)}) %collective-permute-start) | collective-permute-done | bytes 1048608 | tf_op jit(solution)/shard_map/while/body/eval_jaxpr/ppermute | solution.py:14
  165.1 27.4 %collective-permute-done = bf16[16,2,64,256]{3,2,1,0:T(8,128)(2,1)S(1)} collective-permute-done((bf16[16,2,64,256]{3,2,1,0:T(8,128)(2,1)S(1)}, bf16[16,2,64,256]{3,2,1,0:T(8,128)(2,1)S(1)}, u32[]{:S(2)}, u32[]{:S(2)}) %collective-permute-start) | collective-permute-done | bytes 1048608 | tf_op jit(solution)/shard_map/while/body/eval_jaxpr/ppermute | solution.py:14
  198.9 8.9 dynamic_update_slice.15
  208.0 26.5 %collective-permute-done = bf16[16,2,64,256]{3,2,1,0:T(8,128)(2,1)S(1)} collective-permute-done((bf16[16,2,64,256]{3,2,1,0:T(8,128)(2,1)S(1)}, bf16[16,2,64,256]{3,2,1,0:T(8,128)(2,1)S(1)}, u32[]{:S(2)}, u32[]{:S(2)}) %collective-permute-start) | collective-permute-done | bytes 1048608 | tf_op jit(solution)/shard_map/while/body/eval_jaxpr/ppermute | solution.py:14
  247.1 25.5 %collective-permute-done = bf16[16,2,64,256]{3,2,1,0:T(8,128)(2,1)S(1)} collective-permute-done((bf16[16,2,64,256]{3,2,1,0:T(8,128)(2,1)S(1)}, bf16[16,2,64,256]{3,2,1,0:T(8,128)(2,1)S(1)}, u32[]{:S(2)}, u32[]{:S(2)}) %collective-permute-start) | collective-permute-done | bytes 1048608 | tf_op jit(solution)/shard_map/while/body/eval_jaxpr/ppermute | solution.py:14
  279.1 8.8 dynamic_update_slice.15
  288.2 24.6 %collective-permute-done = bf16[16,2,64,256]{3,2,1,0:T(8,128)(2,1)S(1)} collective-permute-done((bf16[16,2,64,256]{3,2,1,0:T(8,128)(2,1)S(1)}, bf16[16,2,64,256]{3,2,1,0:T(8,128)(2,1)S(1)}, u32[]{:S(2)}, u32[]{:S(2)}) %collective-permute-start) | collective-permute-done | bytes 1048608 | tf_op jit(solution)/shard_map/while/body/eval_jaxpr/ppermute | solution.py:14
  325.4 23.7 %collective-permute-done = bf16[16,2,64,256]{3,2,1,0:T(8,128)(2,1)S(1)} collective-permute-done((bf16[16,2,64,256]{3,2,1,0:T(8,128)(2,1)S(1)}, bf16[16,2,64,256]{3,2,1,0:T(8,128)(2,1)S(1)}, u32[]{:S(2)}, u32[]{:S(2)}) %collective-permute-start) | collective-permute-done | bytes 1048608 | tf_op jit(solution)/shard_map/while/body/eval_jaxpr/ppermute | solution.py:14
  355.6 8.8 dynamic_update_slice.15
  364.6 22.8 %collective-permute-done = bf16[16,2,64,256]{3,2,1,0:T(8,128)(2,1)S(1)} collective-permute-done((bf16[16,2,64,256]{3,2,1,0:T(8,128)(2,1)S(1)}, bf16[16,2,64,256]{3,2,1,0:T(8,128)(2,1)S(1)}, u32[]{:S(2)}, u32[]{:S(2)}) %collective-permute-start) | collective-permute-done | bytes 1048608 | tf_op jit(solution)/shard_map/while/body/eval_jaxpr/ppermute | solution.py:14
  400.0 21.9 %collective-permute-done = bf16[16,2,64,256]{3,2,1,0:T(8,128)(2,1)S(1)} collective-permute-done((bf16[16,2,64,256]{3,2,1,0:T(8,128)(2,1)S(1)}, bf16[16,2,64,256]{3,2,1,0:T(8,128)(2,1)S(1)}, u32[]{:S(2)}, u32[]{:S(2)}) %collective-permute-start) | collective-permute-done | bytes 1048608 | tf_op jit(solution)/shard_map/while/body/eval_jaxpr/ppermute | solution.py:14
  428.3 8.9 dynamic_update_slice.15
  437.4 20.9 %collective-permute-done = bf16[16,2,64,256]{3,2,1,0:T(8,128)(2,1)S(1)} collective-permute-done((bf16[16,2,64,256]{3,2,1,0:T(8,128)(2,1)S(1)}, bf16[16,2,64,256]{3,2,1,0:T(8,128)(2,1)S(1)}, u32[]{:S(2)}, u32[]{:S(2)}) %collective-permute-start) | collective-permute-done | bytes 1048608 | tf_op jit(solution)/shard_map/while/body/eval_jaxpr/ppermute | solution.py:14
  471.0 20.0 %collective-permute-done = bf16[16,2,64,256]{3,2,1,0:T(8,128)(2,1)S(1)} collective-permute-done((bf16[16,2,64,256]{3,2,1,0:T(8,128)(2,1)S(1)}, bf16[16,2,64,256]{3,2,1,0:T(8,128)(2,1)S(1)}, u32[]{:S(2)}, u32[]{:S(2)}) %collective-permute-start) | collective-permute-done | bytes 1048608 | tf_op jit(solution)/shard_map/while/body/eval_jaxpr/ppermute | solution.py:14
  497.5 8.9 dynamic_update_slice.15
  506.6 19.1 %collective-permute-done = bf16[16,2,64,256]{3,2,1,0:T(8,128)(2,1)S(1)} collective-permute-done((bf16[16,2,64,256]{3,2,1,0:T(8,128)(2,1)S(1)}, bf16[16,2,64,256]{3,2,1,0:T(8,128)(2,1)S(1)}, u32[]{:S(2)}, u32[]{:S(2)}) %collective-permute-start) | collective-permute-done | bytes 1048608 | tf_op jit(solution)/shard_map/while/body/eval_jaxpr/ppermute | solution.py:14
  538.3 19.0 %collective-permute-done = bf16[16,2,64,256]{3,2,1,0:T(8,128)(2,1)S(1)} collective-permute-done((bf16[16,2,64,256]{3,2,1,0:T(8,128)(2,1)S(1)}, bf16[16,2,64,256]{3,2,1,0:T(8,128)(2,1)S(1)}, u32[]{:S(2)}, u32[]{:S(2)}) %collective-permute-start) | collective-permute-done | bytes 1048608 | tf_op jit(solution)/shard_map/while/body/eval_jaxpr/ppermute | solution.py:14
  563.7 8.9 dynamic_update_slice.15
  572.8 19.0 %collective-permute-done = bf16[16,2,64,256]{3,2,1,0:T(8,128)(2,1)S(1)} collective-permute-done((bf16[16,2,64,256]{3,2,1,0:T(8,128)(2,1)S(1)}, bf16[16,2,64,256]{3,2,1,0:T(8,128)(2,1)S(1)}, u32[]{:S(2)}, u32[]{:S(2)}) %collective-permute-start) | collective-permute-done | bytes 1048608 | tf_op jit(solution)/shard_map/while/body/eval_jaxpr/ppermute | solution.py:14
  604.4 19.0 %collective-permute-done = bf16[16,2,64,256]{3,2,1,0:T(8,128)(2,1)S(1)} collective-permute-done((bf16[16,2,64,256]{3,2,1,0:T(8,128)(2,1)S(1)}, bf16[16,2,64,256]{3,2,1,0:T(8,128)(2,1)S(1)}, u32[]{:S(2)}, u32[]{:S(2)}) %collective-permute-start) | collective-permute-done | bytes 1048608 | tf_op jit(solution)/shard_map/while/body/eval_jaxpr/ppermute | solution.py:14
  629.8 8.9 dynamic_update_slice.15
  638.9 19.0 %collective-permute-done = bf16[16,2,64,256]{3,2,1,0:T(8,128)(2,1)S(1)} collective-permute-done((bf16[16,2,64,256]{3,2,1,0:T(8,128)(2,1)S(1)}, bf16[16,2,64,256]{3,2,1,0:T(8,128)(2,1)S(1)}, u32[]{:S(2)}, u32[]{:S(2)}) %collective-permute-start) | collective-permute-done | bytes 1048608 | tf_op jit(solution)/shard_map/while/body/eval_jaxpr/ppermute | solution.py:14
  670.5 19.0 %collective-permute-done = bf16[16,2,64,256]{3,2,1,0:T(8,128)(2,1)S(1)} collective-permute-done((bf16[16,2,64,256]{3,2,1,0:T(8,128)(2,1)S(1)}, bf16[16,2,64,256]{3,2,1,0:T(8,128)(2,1)S(1)}, u32[]{:S(2)}, u32[]{:S(2)}) %collective-permute-start) | collective-permute-done | bytes 1048608 | tf_op jit(solution)/shard_map/while/body/eval_jaxpr/ppermute | solution.py:14
  696.0 8.9 dynamic_update_slice.15
  705.1 19.0 %collective-permute-done = bf16[16,2,64,256]{3,2,1,0:T(8,128)(2,1)S(1)} collective-permute-done((bf16[16,2,64,256]{3,2,1,0:T(8,128)(2,1)S(1)}, bf16[16,2,64,256]{3,2,1,0:T(8,128)(2,1)S(1)}, u32[]{:S(2)}, u32[]{:S(2)}) %collective-permute-start) | collective-permute-done | bytes 1048608 | tf_op jit(solution)/shard_map/while/body/eval_jaxpr/ppermute | solution.py:14
  736.7 19.0 %collective-permute-done = bf16[16,2,64,256]{3,2,1,0:T(8,128)(2,1)S(1)} collective-permute-done((bf16[16,2,64,256]{3,2,1,0:T(8,128)(2,1)S(1)}, bf16[16,2,64,256]{3,2,1,0:T(8,128)(2,1)S(1)}, u32[]{:S(2)}, u32[]{:S(2)}) %collective-permute-start) | collective-permute-done | bytes 1048608 | tf_op jit(solution)/shard_map/while/body/eval_jaxpr/ppermute | solution.py:14
  762.1 8.9 dynamic_update_slice.15
  771.2 19.8 %collective-permute-done = bf16[16,2,64,256]{3,2,1,0:T(8,128)(2,1)S(1)} collective-permute-done((bf16[16,2,64,256]{3,2,1,0:T(8,128)(2,1)S(1)}, bf16[16,2,64,256]{3,2,1,0:T(8,128)(2,1)S(1)}, u32[]{:S(2)}, u32[]{:S(2)}) %collective-permute-start) | collective-permute-done | bytes 1048608 | tf_op jit(solution)/shard_map/while/body/eval_jaxpr/ppermute | solution.py:14
  803.6 19.0 %collective-permute-done = bf16[16,2,64,256]{3,2,1,0:T(8,128)(2,1)S(1)} collective-permute-done((bf16[16,2,64,256]{3,2,1,0:T(8,128)(2,1)S(1)}, bf16[16,2,64,256]{3,2,1,0:T(8,128)(2,1)S(1)}, u32[]{:S(2)}, u32[]{:S(2)}) %collective-permute-start) | collective-permute-done | bytes 1048608 | tf_op jit(solution)/shard_map/while/body/eval_jaxpr/ppermute | solution.py:14
  838.1 22.0 %collective-permute-done = bf16[16,2,64,256]{3,2,1,0:T(8,128)(2,1)S(1)} collective-permute-done((bf16[16,2,64,256]{3,2,1,0:T(8,128)(2,1)S(1)}, bf16[16,2,64,256]{3,2,1,0:T(8,128)(2,1)S(1)}, u32[]{:S(2)}, u32[]{:S(2)}) %collective-permute-start) | collective-permute-done | bytes 1048608 | tf_op jit(solution)/shard_map/while/body/eval_jaxpr/ppermute | solution.py:14
  872.8 20.2 %collective-permute-done = bf16[16,2,64,256]{3,2,1,0:T(8,128)(2,1)S(1)} collective-permute-done((bf16[16,2,64,256]{3,2,1,0:T(8,128)(2,1)S(1)}, bf16[16,2,64,256]{3,2,1,0:T(8,128)(2,1)S(1)}, u32[]{:S(2)}, u32[]{:S(2)}) %collective-permute-start) | collective-permute-done | bytes 1048608 | tf_op jit(solution)/shard_map/while/body/eval_jaxpr/ppermute | solution.py:14
  908.5 24.2 %collective-permute-done = bf16[16,2,64,256]{3,2,1,0:T(8,128)(2,1)S(1)} collective-permute-done((bf16[16,2,64,256]{3,2,1,0:T(8,128)(2,1)S(1)}, bf16[16,2,64,256]{3,2,1,0:T(8,128)(2,1)S(1)}, u32[]{:S(2)}, u32[]{:S(2)}) %collective-permute-start) | collective-permute-done | bytes 1048608 | tf_op jit(solution)/shard_map/while/body/eval_jaxpr/ppermute | solution.py:14
  945.3 37.0 %collective-permute-done = bf16[16,2,64,256]{3,2,1,0:T(8,128)(2,1)S(1)} collective-permute-done((bf16[16,2,64,256]{3,2,1,0:T(8,128)(2,1)S(1)}, bf16[16,2,64,256]{3,2,1,0:T(8,128)(2,1)S(1)}, u32[]{:S(2)}, u32[]{:S(2)}) %collective-permute-start) | collective-permute-done | bytes 1048608 | tf_op jit(solution)/shard_map/while/body/eval_jaxpr/ppermute | solution.py:14
  988.8 8.9 dynamic_update_slice.15
  997.9 26.6 %collective-permute-done = bf16[16,2,64,256]{3,2,1,0:T(8,128)(2,1)S(1)} collective-permute-done((bf16[16,2,64,256]{3,2,1,0:T(8,128)(2,1)S(1)}, bf16[16,2,64,256]{3,2,1,0:T(8,128)(2,1)S(1)}, u32[]{:S(2)}, u32[]{:S(2)}) %collective-permute-start) | collective-permute-done | bytes 1048608 | tf_op jit(solution)/shard_map/while/body/eval_jaxpr/ppermute | solution.py:14
  1037.1 28.6 %collective-permute-done = bf16[16,2,64,256]{3,2,1,0:T(8,128)(2,1)S(1)} collective-permute-done((bf16[16,2,64,256]{3,2,1,0:T(8,128)(2,1)S(1)}, bf16[16,2,64,256]{3,2,1,0:T(8,128)(2,1)S(1)}, u32[]{:S(2)}, u32[]{:S(2)}) %collective-permute-start) | collective-permute-done | bytes 1048608 | tf_op jit(solution)/shard_map/while/body/eval_jaxpr/ppermute | solution.py:14
  1072.2 8.9 dynamic_update_slice.15
  1081.3 24.8 %collective-permute-done = bf16[16,2,64,256]{3,2,1,0:T(8,128)(2,1)S(1)} collective-permute-done((bf16[16,2,64,256]{3,2,1,0:T(8,128)(2,1)S(1)}, bf16[16,2,64,256]{3,2,1,0:T(8,128)(2,1)S(1)}, u32[]{:S(2)}, u32[]{:S(2)}) %collective-permute-start) | collective-permute-done | bytes 1048608 | tf_op jit(solution)/shard_map/while/body/eval_jaxpr/ppermute | solution.py:14
  1118.7 26.8 %collective-permute-done = bf16[16,2,64,256]{3,2,1,0:T(8,128)(2,1)S(1)} collective-permute-done((bf16[16,2,64,256]{3,2,1,0:T(8,128)(2,1)S(1)}, bf16[16,2,64,256]{3,2,1,0:T(8,128)(2,1)S(1)}, u32[]{:S(2)}, u32[]{:S(2)}) %collective-permute-start) | collective-permute-done | bytes 1048608 | tf_op jit(solution)/shard_map/while/body/eval_jaxpr/ppermute | solution.py:14
  1152.0 8.9 dynamic_update_slice.15
  1161.1 22.9 %collective-permute-done = bf16[16,2,64,256]{3,2,1,0:T(8,128)(2,1)S(1)} collective-permute-done((bf16[16,2,64,256]{3,2,1,0:T(8,128)(2,1)S(1)}, bf16[16,2,64,256]{3,2,1,0:T(8,128)(2,1)S(1)}, u32[]{:S(2)}, u32[]{:S(2)}) %collective-permute-start) | collective-permute-done | bytes 1048608 | tf_op jit(solution)/shard_map/while/body/eval_jaxpr/ppermute | solution.py:14
  1196.6 19.0 %collective-permute-done = bf16[16,2,64,256]{3,2,1,0:T(8,128)(2,1)S(1)} collective-permute-done((bf16[16,2,64,256]{3,2,1,0:T(8,128)(2,1)S(1)}, bf16[16,2,64,256]{3,2,1,0:T(8,128)(2,1)S(1)}, u32[]{:S(2)}, u32[]{:S(2)}) %collective-permute-start) | collective-permute-done | bytes 1048608 | tf_op jit(solution)/shard_map/while/body/eval_jaxpr/ppermute | solution.py:14
  1222.1 8.8 dynamic_update_slice.15
  1231.0 11.8 copy.46
  (387 shorter events, 374.3 us)
Async XLA Ops:
  26.6 20.5 %all-to-all-start = ((bf16[4,2,65536]{2,1,0:T(2,128)(2,1)}), bf16[4,2,65536]{2,1,0:T(2,128)(2,1)S(1)}, u32[]{:S(2)}, u32[]{:S(2)}) async-start(bf16[4,2,65536]{2,1,0:T(2,128)(2,1)} %reshape.341), calls=%async_computation | async-start | bytes 2097152 | tf_op jit(solution)/shard_map/all_to_all | solution.py:70
  78.3 31.7 %collective-permute-start = (bf16[16,2,64,256]{3,2,1,0:T(8,128)(2,1)S(1)}, bf16[16,2,64,256]{3,2,1,0:T(8,128)(2,1)S(1)}, u32[]{:S(2)}, u32[]{:S(2)}) collective-permute-start(bf16[16,2,64,256]{3,2,1,0:T(8,128)(2,1)S(1)} %get-tuple-element.220), channel_id=1, source_target_pairs={{124,0},{0,4},{4,8},{8,12},{12,16},{16,20},{20,24},{24,28},{28,32}... | collective-permute-start | bytes 3145736 | tf_op jit(solution)/shard_map/while/body/eval_jaxpr/ppermute | solution.py:14
  113.9 10.7 copy-start.1
  124.7 28.4 %collective-permute-start = (bf16[16,2,64,256]{3,2,1,0:T(8,128)(2,1)S(1)}, bf16[16,2,64,256]{3,2,1,0:T(8,128)(2,1)S(1)}, u32[]{:S(2)}, u32[]{:S(2)}) collective-permute-start(bf16[16,2,64,256]{3,2,1,0:T(8,128)(2,1)S(1)} %get-tuple-element.220), channel_id=1, source_target_pairs={{124,0},{0,4},{4,8},{8,12},{12,16},{16,20},{20,24},{24,28},{28,32}... | collective-permute-start | bytes 3145736 | tf_op jit(solution)/shard_map/while/body/eval_jaxpr/ppermute | solution.py:14
  165.0 27.5 %collective-permute-start = (bf16[16,2,64,256]{3,2,1,0:T(8,128)(2,1)S(1)}, bf16[16,2,64,256]{3,2,1,0:T(8,128)(2,1)S(1)}, u32[]{:S(2)}, u32[]{:S(2)}) collective-permute-start(bf16[16,2,64,256]{3,2,1,0:T(8,128)(2,1)S(1)} %get-tuple-element.220), channel_id=1, source_target_pairs={{124,0},{0,4},{4,8},{8,12},{12,16},{16,20},{20,24},{24,28},{28,32}... | collective-permute-start | bytes 3145736 | tf_op jit(solution)/shard_map/while/body/eval_jaxpr/ppermute | solution.py:14
  196.2 11.5 copy-start.1
  207.9 26.6 %collective-permute-start = (bf16[16,2,64,256]{3,2,1,0:T(8,128)(2,1)S(1)}, bf16[16,2,64,256]{3,2,1,0:T(8,128)(2,1)S(1)}, u32[]{:S(2)}, u32[]{:S(2)}) collective-permute-start(bf16[16,2,64,256]{3,2,1,0:T(8,128)(2,1)S(1)} %get-tuple-element.220), channel_id=1, source_target_pairs={{124,0},{0,4},{4,8},{8,12},{12,16},{16,20},{20,24},{24,28},{28,32}... | collective-permute-start | bytes 3145736 | tf_op jit(solution)/shard_map/while/body/eval_jaxpr/ppermute | solution.py:14
  247.0 25.6 %collective-permute-start = (bf16[16,2,64,256]{3,2,1,0:T(8,128)(2,1)S(1)}, bf16[16,2,64,256]{3,2,1,0:T(8,128)(2,1)S(1)}, u32[]{:S(2)}, u32[]{:S(2)}) collective-permute-start(bf16[16,2,64,256]{3,2,1,0:T(8,128)(2,1)S(1)} %get-tuple-element.220), channel_id=1, source_target_pairs={{124,0},{0,4},{4,8},{8,12},{12,16},{16,20},{20,24},{24,28},{28,32}... | collective-permute-start | bytes 3145736 | tf_op jit(solution)/shard_map/while/body/eval_jaxpr/ppermute | solution.py:14
  276.4 11.5 copy-start.1
  288.1 24.7 %collective-permute-start = (bf16[16,2,64,256]{3,2,1,0:T(8,128)(2,1)S(1)}, bf16[16,2,64,256]{3,2,1,0:T(8,128)(2,1)S(1)}, u32[]{:S(2)}, u32[]{:S(2)}) collective-permute-start(bf16[16,2,64,256]{3,2,1,0:T(8,128)(2,1)S(1)} %get-tuple-element.220), channel_id=1, source_target_pairs={{124,0},{0,4},{4,8},{8,12},{12,16},{16,20},{20,24},{24,28},{28,32}... | collective-permute-start | bytes 3145736 | tf_op jit(solution)/shard_map/while/body/eval_jaxpr/ppermute | solution.py:14
  325.3 23.8 %collective-permute-start = (bf16[16,2,64,256]{3,2,1,0:T(8,128)(2,1)S(1)}, bf16[16,2,64,256]{3,2,1,0:T(8,128)(2,1)S(1)}, u32[]{:S(2)}, u32[]{:S(2)}) collective-permute-start(bf16[16,2,64,256]{3,2,1,0:T(8,128)(2,1)S(1)} %get-tuple-element.220), channel_id=1, source_target_pairs={{124,0},{0,4},{4,8},{8,12},{12,16},{16,20},{20,24},{24,28},{28,32}... | collective-permute-start | bytes 3145736 | tf_op jit(solution)/shard_map/while/body/eval_jaxpr/ppermute | solution.py:14
  352.9 11.5 copy-start.1
  364.5 22.9 %collective-permute-start = (bf16[16,2,64,256]{3,2,1,0:T(8,128)(2,1)S(1)}, bf16[16,2,64,256]{3,2,1,0:T(8,128)(2,1)S(1)}, u32[]{:S(2)}, u32[]{:S(2)}) collective-permute-start(bf16[16,2,64,256]{3,2,1,0:T(8,128)(2,1)S(1)} %get-tuple-element.220), channel_id=1, source_target_pairs={{124,0},{0,4},{4,8},{8,12},{12,16},{16,20},{20,24},{24,28},{28,32}... | collective-permute-start | bytes 3145736 | tf_op jit(solution)/shard_map/while/body/eval_jaxpr/ppermute | solution.py:14
  399.9 22.0 %collective-permute-start = (bf16[16,2,64,256]{3,2,1,0:T(8,128)(2,1)S(1)}, bf16[16,2,64,256]{3,2,1,0:T(8,128)(2,1)S(1)}, u32[]{:S(2)}, u32[]{:S(2)}) collective-permute-start(bf16[16,2,64,256]{3,2,1,0:T(8,128)(2,1)S(1)} %get-tuple-element.220), channel_id=1, source_target_pairs={{124,0},{0,4},{4,8},{8,12},{12,16},{16,20},{20,24},{24,28},{28,32}... | collective-permute-start | bytes 3145736 | tf_op jit(solution)/shard_map/while/body/eval_jaxpr/ppermute | solution.py:14
  425.7 11.5 copy-start.1
  437.3 21.0 %collective-permute-start = (bf16[16,2,64,256]{3,2,1,0:T(8,128)(2,1)S(1)}, bf16[16,2,64,256]{3,2,1,0:T(8,128)(2,1)S(1)}, u32[]{:S(2)}, u32[]{:S(2)}) collective-permute-start(bf16[16,2,64,256]{3,2,1,0:T(8,128)(2,1)S(1)} %get-tuple-element.220), channel_id=1, source_target_pairs={{124,0},{0,4},{4,8},{8,12},{12,16},{16,20},{20,24},{24,28},{28,32}... | collective-permute-start | bytes 3145736 | tf_op jit(solution)/shard_map/while/body/eval_jaxpr/ppermute | solution.py:14
  470.9 20.1 %collective-permute-start = (bf16[16,2,64,256]{3,2,1,0:T(8,128)(2,1)S(1)}, bf16[16,2,64,256]{3,2,1,0:T(8,128)(2,1)S(1)}, u32[]{:S(2)}, u32[]{:S(2)}) collective-permute-start(bf16[16,2,64,256]{3,2,1,0:T(8,128)(2,1)S(1)} %get-tuple-element.220), channel_id=1, source_target_pairs={{124,0},{0,4},{4,8},{8,12},{12,16},{16,20},{20,24},{24,28},{28,32}... | collective-permute-start | bytes 3145736 | tf_op jit(solution)/shard_map/while/body/eval_jaxpr/ppermute | solution.py:14
  494.8 11.5 copy-start.1
  506.5 19.2 %collective-permute-start = (bf16[16,2,64,256]{3,2,1,0:T(8,128)(2,1)S(1)}, bf16[16,2,64,256]{3,2,1,0:T(8,128)(2,1)S(1)}, u32[]{:S(2)}, u32[]{:S(2)}) collective-permute-start(bf16[16,2,64,256]{3,2,1,0:T(8,128)(2,1)S(1)} %get-tuple-element.220), channel_id=1, source_target_pairs={{124,0},{0,4},{4,8},{8,12},{12,16},{16,20},{20,24},{24,28},{28,32}... | collective-permute-start | bytes 3145736 | tf_op jit(solution)/shard_map/while/body/eval_jaxpr/ppermute | solution.py:14
  538.2 19.1 %collective-permute-start = (bf16[16,2,64,256]{3,2,1,0:T(8,128)(2,1)S(1)}, bf16[16,2,64,256]{3,2,1,0:T(8,128)(2,1)S(1)}, u32[]{:S(2)}, u32[]{:S(2)}) collective-permute-start(bf16[16,2,64,256]{3,2,1,0:T(8,128)(2,1)S(1)} %get-tuple-element.220), channel_id=1, source_target_pairs={{124,0},{0,4},{4,8},{8,12},{12,16},{16,20},{20,24},{24,28},{28,32}... | collective-permute-start | bytes 3145736 | tf_op jit(solution)/shard_map/while/body/eval_jaxpr/ppermute | solution.py:14
  561.0 11.5 copy-start.1
  572.7 19.1 %collective-permute-start = (bf16[16,2,64,256]{3,2,1,0:T(8,128)(2,1)S(1)}, bf16[16,2,64,256]{3,2,1,0:T(8,128)(2,1)S(1)}, u32[]{:S(2)}, u32[]{:S(2)}) collective-permute-start(bf16[16,2,64,256]{3,2,1,0:T(8,128)(2,1)S(1)} %get-tuple-element.220), channel_id=1, source_target_pairs={{124,0},{0,4},{4,8},{8,12},{12,16},{16,20},{20,24},{24,28},{28,32}... | collective-permute-start | bytes 3145736 | tf_op jit(solution)/shard_map/while/body/eval_jaxpr/ppermute | solution.py:14
  604.3 19.1 %collective-permute-start = (bf16[16,2,64,256]{3,2,1,0:T(8,128)(2,1)S(1)}, bf16[16,2,64,256]{3,2,1,0:T(8,128)(2,1)S(1)}, u32[]{:S(2)}, u32[]{:S(2)}) collective-permute-start(bf16[16,2,64,256]{3,2,1,0:T(8,128)(2,1)S(1)} %get-tuple-element.220), channel_id=1, source_target_pairs={{124,0},{0,4},{4,8},{8,12},{12,16},{16,20},{20,24},{24,28},{28,32}... | collective-permute-start | bytes 3145736 | tf_op jit(solution)/shard_map/while/body/eval_jaxpr/ppermute | solution.py:14
  627.2 11.5 copy-start.1
  638.8 19.1 %collective-permute-start = (bf16[16,2,64,256]{3,2,1,0:T(8,128)(2,1)S(1)}, bf16[16,2,64,256]{3,2,1,0:T(8,128)(2,1)S(1)}, u32[]{:S(2)}, u32[]{:S(2)}) collective-permute-start(bf16[16,2,64,256]{3,2,1,0:T(8,128)(2,1)S(1)} %get-tuple-element.220), channel_id=1, source_target_pairs={{124,0},{0,4},{4,8},{8,12},{12,16},{16,20},{20,24},{24,28},{28,32}... | collective-permute-start | bytes 3145736 | tf_op jit(solution)/shard_map/while/body/eval_jaxpr/ppermute | solution.py:14
  670.4 19.1 %collective-permute-start = (bf16[16,2,64,256]{3,2,1,0:T(8,128)(2,1)S(1)}, bf16[16,2,64,256]{3,2,1,0:T(8,128)(2,1)S(1)}, u32[]{:S(2)}, u32[]{:S(2)}) collective-permute-start(bf16[16,2,64,256]{3,2,1,0:T(8,128)(2,1)S(1)} %get-tuple-element.220), channel_id=1, source_target_pairs={{124,0},{0,4},{4,8},{8,12},{12,16},{16,20},{20,24},{24,28},{28,32}... | collective-permute-start | bytes 3145736 | tf_op jit(solution)/shard_map/while/body/eval_jaxpr/ppermute | solution.py:14
  693.3 11.5 copy-start.1
  704.9 19.1 %collective-permute-start = (bf16[16,2,64,256]{3,2,1,0:T(8,128)(2,1)S(1)}, bf16[16,2,64,256]{3,2,1,0:T(8,128)(2,1)S(1)}, u32[]{:S(2)}, u32[]{:S(2)}) collective-permute-start(bf16[16,2,64,256]{3,2,1,0:T(8,128)(2,1)S(1)} %get-tuple-element.220), channel_id=1, source_target_pairs={{124,0},{0,4},{4,8},{8,12},{12,16},{16,20},{20,24},{24,28},{28,32}... | collective-permute-start | bytes 3145736 | tf_op jit(solution)/shard_map/while/body/eval_jaxpr/ppermute | solution.py:14
  736.6 19.1 %collective-permute-start = (bf16[16,2,64,256]{3,2,1,0:T(8,128)(2,1)S(1)}, bf16[16,2,64,256]{3,2,1,0:T(8,128)(2,1)S(1)}, u32[]{:S(2)}, u32[]{:S(2)}) collective-permute-start(bf16[16,2,64,256]{3,2,1,0:T(8,128)(2,1)S(1)} %get-tuple-element.220), channel_id=1, source_target_pairs={{124,0},{0,4},{4,8},{8,12},{12,16},{16,20},{20,24},{24,28},{28,32}... | collective-permute-start | bytes 3145736 | tf_op jit(solution)/shard_map/while/body/eval_jaxpr/ppermute | solution.py:14
  759.5 11.5 copy-start.1
  771.1 19.9 %collective-permute-start = (bf16[16,2,64,256]{3,2,1,0:T(8,128)(2,1)S(1)}, bf16[16,2,64,256]{3,2,1,0:T(8,128)(2,1)S(1)}, u32[]{:S(2)}, u32[]{:S(2)}) collective-permute-start(bf16[16,2,64,256]{3,2,1,0:T(8,128)(2,1)S(1)} %get-tuple-element.220), channel_id=1, source_target_pairs={{124,0},{0,4},{4,8},{8,12},{12,16},{16,20},{20,24},{24,28},{28,32}... | collective-permute-start | bytes 3145736 | tf_op jit(solution)/shard_map/while/body/eval_jaxpr/ppermute | solution.py:14
  803.5 19.1 %collective-permute-start = (bf16[16,2,64,256]{3,2,1,0:T(8,128)(2,1)S(1)}, bf16[16,2,64,256]{3,2,1,0:T(8,128)(2,1)S(1)}, u32[]{:S(2)}, u32[]{:S(2)}) collective-permute-start(bf16[16,2,64,256]{3,2,1,0:T(8,128)(2,1)S(1)} %get-tuple-element.220), channel_id=1, source_target_pairs={{124,0},{0,4},{4,8},{8,12},{12,16},{16,20},{20,24},{24,28},{28,32}... | collective-permute-start | bytes 3145736 | tf_op jit(solution)/shard_map/while/body/eval_jaxpr/ppermute | solution.py:14
  826.4 11.5 copy-start.1
  838.0 22.1 %collective-permute-start = (bf16[16,2,64,256]{3,2,1,0:T(8,128)(2,1)S(1)}, bf16[16,2,64,256]{3,2,1,0:T(8,128)(2,1)S(1)}, u32[]{:S(2)}, u32[]{:S(2)}) collective-permute-start(bf16[16,2,64,256]{3,2,1,0:T(8,128)(2,1)S(1)} %get-tuple-element.220), channel_id=1, source_target_pairs={{124,0},{0,4},{4,8},{8,12},{12,16},{16,20},{20,24},{24,28},{28,32}... | collective-permute-start | bytes 3145736 | tf_op jit(solution)/shard_map/while/body/eval_jaxpr/ppermute | solution.py:14
  872.7 20.3 %collective-permute-start = (bf16[16,2,64,256]{3,2,1,0:T(8,128)(2,1)S(1)}, bf16[16,2,64,256]{3,2,1,0:T(8,128)(2,1)S(1)}, u32[]{:S(2)}, u32[]{:S(2)}) collective-permute-start(bf16[16,2,64,256]{3,2,1,0:T(8,128)(2,1)S(1)} %get-tuple-element.220), channel_id=1, source_target_pairs={{124,0},{0,4},{4,8},{8,12},{12,16},{16,20},{20,24},{24,28},{28,32}... | collective-permute-start | bytes 3145736 | tf_op jit(solution)/shard_map/while/body/eval_jaxpr/ppermute | solution.py:14
  896.8 11.5 copy-start.1
  908.4 24.3 %collective-permute-start = (bf16[16,2,64,256]{3,2,1,0:T(8,128)(2,1)S(1)}, bf16[16,2,64,256]{3,2,1,0:T(8,128)(2,1)S(1)}, u32[]{:S(2)}, u32[]{:S(2)}) collective-permute-start(bf16[16,2,64,256]{3,2,1,0:T(8,128)(2,1)S(1)} %get-tuple-element.220), channel_id=1, source_target_pairs={{124,0},{0,4},{4,8},{8,12},{12,16},{16,20},{20,24},{24,28},{28,32}... | collective-permute-start | bytes 3145736 | tf_op jit(solution)/shard_map/while/body/eval_jaxpr/ppermute | solution.py:14
  945.2 37.1 %collective-permute-start = (bf16[16,2,64,256]{3,2,1,0:T(8,128)(2,1)S(1)}, bf16[16,2,64,256]{3,2,1,0:T(8,128)(2,1)S(1)}, u32[]{:S(2)}, u32[]{:S(2)}) collective-permute-start(bf16[16,2,64,256]{3,2,1,0:T(8,128)(2,1)S(1)} %get-tuple-element.220), channel_id=1, source_target_pairs={{124,0},{0,4},{4,8},{8,12},{12,16},{16,20},{20,24},{24,28},{28,32}... | collective-permute-start | bytes 3145736 | tf_op jit(solution)/shard_map/while/body/eval_jaxpr/ppermute | solution.py:14
  986.1 11.5 copy-start.1
  997.8 26.7 %collective-permute-start = (bf16[16,2,64,256]{3,2,1,0:T(8,128)(2,1)S(1)}, bf16[16,2,64,256]{3,2,1,0:T(8,128)(2,1)S(1)}, u32[]{:S(2)}, u32[]{:S(2)}) collective-permute-start(bf16[16,2,64,256]{3,2,1,0:T(8,128)(2,1)S(1)} %get-tuple-element.220), channel_id=1, source_target_pairs={{124,0},{0,4},{4,8},{8,12},{12,16},{16,20},{20,24},{24,28},{28,32}... | collective-permute-start | bytes 3145736 | tf_op jit(solution)/shard_map/while/body/eval_jaxpr/ppermute | solution.py:14
  1037.0 28.8 %collective-permute-start = (bf16[16,2,64,256]{3,2,1,0:T(8,128)(2,1)S(1)}, bf16[16,2,64,256]{3,2,1,0:T(8,128)(2,1)S(1)}, u32[]{:S(2)}, u32[]{:S(2)}) collective-permute-start(bf16[16,2,64,256]{3,2,1,0:T(8,128)(2,1)S(1)} %get-tuple-element.220), channel_id=1, source_target_pairs={{124,0},{0,4},{4,8},{8,12},{12,16},{16,20},{20,24},{24,28},{28,32}... | collective-permute-start | bytes 3145736 | tf_op jit(solution)/shard_map/while/body/eval_jaxpr/ppermute | solution.py:14
  1069.5 11.5 copy-start.1
  1081.2 24.9 %collective-permute-start = (bf16[16,2,64,256]{3,2,1,0:T(8,128)(2,1)S(1)}, bf16[16,2,64,256]{3,2,1,0:T(8,128)(2,1)S(1)}, u32[]{:S(2)}, u32[]{:S(2)}) collective-permute-start(bf16[16,2,64,256]{3,2,1,0:T(8,128)(2,1)S(1)} %get-tuple-element.220), channel_id=1, source_target_pairs={{124,0},{0,4},{4,8},{8,12},{12,16},{16,20},{20,24},{24,28},{28,32}... | collective-permute-start | bytes 3145736 | tf_op jit(solution)/shard_map/while/body/eval_jaxpr/ppermute | solution.py:14
  1118.6 26.9 %collective-permute-start = (bf16[16,2,64,256]{3,2,1,0:T(8,128)(2,1)S(1)}, bf16[16,2,64,256]{3,2,1,0:T(8,128)(2,1)S(1)}, u32[]{:S(2)}, u32[]{:S(2)}) collective-permute-start(bf16[16,2,64,256]{3,2,1,0:T(8,128)(2,1)S(1)} %get-tuple-element.220), channel_id=1, source_target_pairs={{124,0},{0,4},{4,8},{8,12},{12,16},{16,20},{20,24},{24,28},{28,32}... | collective-permute-start | bytes 3145736 | tf_op jit(solution)/shard_map/while/body/eval_jaxpr/ppermute | solution.py:14
  1149.3 11.5 copy-start.1
  1161.0 23.0 %collective-permute-start = (bf16[16,2,64,256]{3,2,1,0:T(8,128)(2,1)S(1)}, bf16[16,2,64,256]{3,2,1,0:T(8,128)(2,1)S(1)}, u32[]{:S(2)}, u32[]{:S(2)}) collective-permute-start(bf16[16,2,64,256]{3,2,1,0:T(8,128)(2,1)S(1)} %get-tuple-element.220), channel_id=1, source_target_pairs={{124,0},{0,4},{4,8},{8,12},{12,16},{16,20},{20,24},{24,28},{28,32}... | collective-permute-start | bytes 3145736 | tf_op jit(solution)/shard_map/while/body/eval_jaxpr/ppermute | solution.py:14
  1196.5 19.1 %collective-permute-start = (bf16[16,2,64,256]{3,2,1,0:T(8,128)(2,1)S(1)}, bf16[16,2,64,256]{3,2,1,0:T(8,128)(2,1)S(1)}, u32[]{:S(2)}, u32[]{:S(2)}) collective-permute-start(bf16[16,2,64,256]{3,2,1,0:T(8,128)(2,1)S(1)} %get-tuple-element.220), channel_id=1, source_target_pairs={{124,0},{0,4},{4,8},{8,12},{12,16},{16,20},{20,24},{24,28},{28,32}... | collective-permute-start | bytes 3145736 | tf_op jit(solution)/shard_map/while/body/eval_jaxpr/ppermute | solution.py:14
  1219.4 11.5 copy-start.1
  (46 other events, 158.4 us)
where the time goes:
time: 1250 us; the launch traced here: 1240 us
  waiting for transfers between devices  728 us (58%)
  local copies, waits for them, and re-layouts  418 us (33%)
  matrix products  59 us (5%)
  other arithmetic  24.1 us (2%)
    ppermute x31, waiting for transfers between devices, passed_along(): return lax.ppermute(block, axis, route)  712 us
    dynamic_update_slice x32, local copies, waits for them, and re-layouts, place_block(): return lax.dynamic_update_slice(result, block, (0, 0, 0, column_first))  235 us
    slice x32, local copies, waits for them, and re-layouts, cross_block(): real_part = products[:, 0, :, 0] + products[:, 1, :, 1]  74.6 us
    dot_general x32, matrix products, cross_block(): jnp.einsum('fcw,fdw->fcd', own_panel.reshape(bin_count, 2 * row_count, wi...  52.7 us
    reshape x32, local copies, waits for them, and re-layouts, cross_block(): products = products.reshape(bin_count, 2, row_count, 2, col_count)  38.7 us
    while x155, local copies, waits for them, and re-layouts  33.3 us
  transfers between devices with their start and end apart: 32, of which 32 were waited for; matrix products, arithmetic and copies ran while one was open for 0% of the time, Pallas kernels for 0%

commit v1 on v0

v1 whole, which is shorter than its diff:
```python
import math

import jax
import jax.numpy as jnp
from jax import lax
from jax.sharding import PartitionSpec as P

CLIP_FACTOR = 2.0


def dft_table(freq_bins, length):
    samples = jnp.arange(length, dtype=jnp.int32)
    phase_index = samples[:, None] * freq_bins[None, :] % length
    angle = phase_index.astype(jnp.float32) * (2.0 * math.pi / length)
    taper = 0.5 - 0.5 * jnp.cos(samples.astype(jnp.float32) * (2.0 * math.pi / length))
    cosine = taper[:, None] * jnp.cos(angle)
    sine = -taper[:, None] * jnp.sin(angle)
    stacked = jnp.stack([cosine, sine], axis=2)
    return stacked.reshape(length, 2 * freq_bins.shape[0]).astype(jnp.bfloat16)


def clip_scales(mad_index, mad_table):
    entries = jnp.arange(mad_table.shape[0], dtype=jnp.int32)
    matches = mad_index[:, None] == entries[None, :]
    return jnp.sum(jnp.where(matches, mad_table[None, :], 0.0), axis=1)


def row_operand(panel):
    first, second = panel[:, 0], panel[:, 1]
    real_rows = jnp.stack([first, second], axis=2)
    imag_rows = jnp.stack([second, -first], axis=2)
    return jnp.stack([real_rows, imag_rows], axis=1)


def per_device(strain, mad_index, mad_table, freq_bins, valid_count):
    channels, win_local, length = strain.shape
    bin_count = freq_bins.shape[0]
    limits = (clip_scales(mad_index, mad_table) * CLIP_FACTOR)[:, None, None]
    clipped = jnp.clip(strain.astype(jnp.float32), -limits, limits).astype(jnp.bfloat16)
    table = dft_table(freq_bins, length)
    flat_rows = clipped.reshape(channels * win_local, length)
    spectrum = lax.dot_general(
        table, flat_rows, (((0,), (1,)), ((), ())), preferred_element_type=jnp.float32
    )
    window_ids = lax.axis_index("freq") * win_local + jnp.arange(win_local, dtype=jnp.int32)
    counts = valid_count.astype(jnp.float32)
    weights = jnp.where(
        window_ids[None, :] < valid_count[:, None], 1.0 / jnp.sqrt(counts)[:, None], 0.0
    )
    weighted = (spectrum * weights.reshape(1, channels * win_local)).astype(jnp.bfloat16)
    weighted = weighted.reshape(bin_count, 2, channels, win_local)
    panels = lax.all_to_all(weighted, "freq", split_axis=0, concat_axis=3, tiled=True)
    columns = lax.all_gather(panels, "chan", axis=2, tiled=True)
    rows = row_operand(panels)
    return jnp.einsum(
        "fqipw,fpjw->fqij", rows, columns, preferred_element_type=jnp.float32
    )


def solution(mesh):
    return jax.shard_map(
        per_device,
        mesh=mesh,
        in_specs=(P("chan", "freq", None), P("chan"), P(), P(), P("chan")),
        out_specs=P("freq", None, "chan", None),
        check_vma=False,
    )
```

time: 1250 us -> 458 us (0.37)
  local copies, waits for them, and re-layouts: 418 us -> 16.4 us
  waiting for transfers between devices: 728 us -> 362 us
  matrix products: 59 us -> 28.2 us
  blocking collectives: 0 us -> 20.4 us
  between operations: 0.13 us -> 13.5 us
    ppermute x31 -> x0, waiting for transfers between devices: 712 us -> none  [passed_along(): return lax.ppermute(block, axis, route)]
    all_gather x0 -> x1, waiting for transfers between devices: none -> 362 us  [per_device(): columns = lax.all_gather(panels, 'chan', axis=2, tiled=True)]
    dynamic_update_slice x32 -> x0, local copies, waits for them, and re-layouts: 235 us -> none  [place_block(): return lax.dynamic_update_slice(result, block, (0, 0, 0, column_first))]
    slice x32 -> x0, local copies, waits for them, and re-layouts: 74.6 us -> none  [cross_block(): real_part = products[:, 0, :, 0] + products[:, 1, :, 1]]
    while x156 -> x0, local copies, waits for them, and re-layouts: 45.2 us -> none
    reshape x33 -> x0, local copies, waits for them, and re-layouts: 40 us -> none  [the longest x32 38.7 us: cross_block(): products = products.reshape(bin_count, 2, row_count, 2, col_count)]
    dot_general x32 -> x1, matrix products: 52.7 us -> 22 us  [per_device(): jnp.einsum('fqipw,fpjw->fqij', rows, columns, preferred_element_type=jnp....]
    all_to_all x0 -> x1, blocking collectives: none -> 20.4 us  [per_device(): lax.all_to_all(weighted, 'freq', split_axis=0, concat_axis=3, tiled=True)]
  transfers between devices with their start and end apart: 32 -> 1, of which waited for: 32 -> 1; matrix products, arithmetic and copies ran while one was open for 0% -> 1% of each run, Pallas kernels for 0% -> 0%
where the time goes in v1:
time: 458 us; the launch traced here: 457 us
  waiting for transfers between devices  362 us (79%)
  matrix products  28.2 us (6%)
  blocking collectives  20.4 us (4%)
  local copies, waits for them, and re-layouts  16.4 us (4%)
  other arithmetic  16.2 us (4%)
  between operations  13.5 us (3%)
    all_gather x1, waiting for transfers between devices, per_device(): columns = lax.all_gather(panels, 'chan', axis=2, tiled=True)  362 us
    dot_general x1, matrix products, per_device(): jnp.einsum('fqipw,fpjw->fqij', rows, columns, preferred_element_type=jnp....  22 us
    all_to_all x1, blocking collectives, per_device(): lax.all_to_all(weighted, 'freq', split_axis=0, concat_axis=3, tiled=True)  20.4 us
    convert_element_type x1, other arithmetic, per_device(): jnp.clip(strain.astype(jnp.float32), -limits, limits).astype(jnp.bfloat16)  10.8 us
  transfers between devices with their start and end apart: 1, of which 1 were waited for; matrix products, arithmetic and copies ran while one was open for 1% of the time, Pallas kernels for 0%

profile of v1, /device:TPU:0, one launch (start us, length us, event | category | flops | bytes accessed | tf_op | source)
XLA Modules:
  0.0 457.1 jit_solution(5203955998061917889)
XLA Ops:
  6.5 0.0 all-gather.2.cloned.1.call-start
  6.6 0.7 convert_rsqrt_fusion
  7.3 0.8 select_reduce_fusion
  8.0 0.7 compare_select_fusion
  8.8 0.1 select_n.36
  8.8 1.9 multiply_convert_fusion.1
  10.8 0.3 copy.15
  11.1 0.1 convert_element_type.50
  11.2 10.8 %minimum_convert_fusion = bf16[64,64,1024]{2,1,0:T(8,128)(2,1)} fusion(bf16[64,64,1024]{2,1,0:T(8,128)(2,1)} %param.5, bf16[64]{0:T(256)(128)(2,1)S(1)} %get-tuple-element.10, bf16[64]{0:T(256)(128)(2,1)S(1)} %get-tuple-element.9), kind=kLoop, calls=%fused_computation.2 | loop fusion | flops 25165824 | bytes 16777472 | tf_op jit(solution)/shard_map/convert_element_type | solution.py:39
  21.9 6.3 %fusion.5 = bf16[128,4096]{1,0:T(8,128)(2,1)S(1)} fusion(bf16[1024,128]{0,1:T(8,128)(2,1)S(1)} %convert_element_type.50, bf16[4096,1024]{1,0:T(8,128)(2,1)} %bitcast.31, f32[4096]{0:T(1024)S(1)} %select_n.36), kind=kOutput, calls=%fused_computation.5 | convolution fusion | flops 1074790400 | bytes 9715712 | tf_op jit(solution)/shard_map/dot_general | solution.py:42
  28.2 2.3 reshape.218
  30.5 1.7 reshape.221
  32.2 20.4 %all_to_all.18 = bf16[4,2,65536]{2,1,0:T(2,128)(2,1)} all-to-all(bf16[4,2,65536]{2,1,0:T(2,128)(2,1)S(1)} %reshape.221), channel_id=1, replica_groups=mesh['chan'=32,'freq'=4] {'freq'}, dimensions={0} | all-to-all | bytes 2097152 | tf_op jit(solution)/shard_map/all_to_all | solution.py:52
  52.6 3.1 reshape.222
  55.7 3.3 copy.25
  59.0 4.4 all_to_all.16
  63.3 0.0 all-gather.2.cloned.1.call-update
  63.4 1.1 fusion.15
  64.4 1.3 slice_bitcast_fusion.1
  65.7 0.2 maximum_bitcast_fusion
  65.9 362.3 %all-gather.2.cloned.1.call-done = bf16[16,2,2048,256]{3,2,1,0:T(8,128)(2,1)} async-done(((bf16[16,2,64,256]{3,2,1,0:T(8,128)(2,1)}), bf16[16,2,2048,256]{3,2,1,0:T(8,128)(2,1)}) %all-gather.2.cloned.1.call-update) | async-done | bytes 33554448 | tf_op jit(solution)/shard_map/all_gather | solution.py:53
  428.2 22.0 %fusion.2 = f32[16,2,64,2048]{3,2,1,0:T(8,128)} fusion(bf16[16,2,2048,256]{3,2,1,0:T(8,128)(2,1)} %all-gather.2.cloned.1.call-done, bf16[16,1,64,2,256]{4,2,0,3,1:T(8,128)(2,1)S(1)} %get-tuple-element.8, bf16[16,1,64,2,256]{4,2,0,3,1:T(8,128)(2,1)S(1)} %get-tuple-element.7), kind=kOutput, calls=%fused_computation.3 | convolution fusion | flops 4296015872 | bytes 52428800 | tf_op jit(solution)/shard_map/fqipw,fpjw->fqij/dot_general | solution.py:55
  (4 shorter events, 0.1 us)
Async XLA Ops:
  6.5 421.7 %all-gather.2.cloned.1.call-start = ((), (), s32[]{:S(2)}) async-start(), calls=%async_computation.1 | async-start | bytes 34603008 | tf_op jit(solution)/shard_map/all_gather | solution.py:53
Sparse Core Ops, SparseCore 0:
  63.5 364.7 all-gather.1

commit v2 on v1

--- a/solution.py
+++ b/solution.py
@@ -3,7 +3,7 @@
 import jax
 import jax.numpy as jnp
 from jax import lax
-from jax.sharding import PartitionSpec as P
+from jax.sharding import Mesh, PartitionSpec as P
 
 CLIP_FACTOR = 2.0
 
@@ -32,6 +32,21 @@
     return jnp.stack([real_rows, imag_rows], axis=1)
 
 
+def shifted(block, axis, distance):
+    size = lax.axis_size(axis)
+    return lax.ppermute(block, axis, [((i + distance) % size, i) for i in range(size)])
+
+
+def ring_gather(block, axis, split_axis):
+    ahead = shifted(block, axis, 1)
+    behind = shifted(block, axis, -1)
+    half = block.shape[split_axis] // 2
+    far_a = shifted(lax.slice_in_dim(ahead, 0, half, axis=split_axis), axis, 1)
+    far_b = shifted(lax.slice_in_dim(behind, half, 2 * half, axis=split_axis), axis, -1)
+    far = jnp.concatenate([far_a, far_b], axis=split_axis)
+    return [block, ahead, far, behind]
+
+
 def per_device(strain, mad_index, mad_table, freq_bins, valid_count):
     channels, win_local, length = strain.shape
     bin_count = freq_bins.shape[0]
@@ -42,26 +57,59 @@
     spectrum = lax.dot_general(
         table, flat_rows, (((0,), (1,)), ((), ())), preferred_element_type=jnp.float32
     )
-    window_ids = lax.axis_index("freq") * win_local + jnp.arange(win_local, dtype=jnp.int32)
+    freq_index = lax.axis_index("yhi") * lax.axis_size("core") + lax.axis_index("core")
+    window_ids = freq_index * win_local + jnp.arange(win_local, dtype=jnp.int32)
     counts = valid_count.astype(jnp.float32)
     weights = jnp.where(
         window_ids[None, :] < valid_count[:, None], 1.0 / jnp.sqrt(counts)[:, None], 0.0
     )
     weighted = (spectrum * weights.reshape(1, channels * win_local)).astype(jnp.bfloat16)
-    weighted = weighted.reshape(bin_count, 2, channels, win_local)
-    panels = lax.all_to_all(weighted, "freq", split_axis=0, concat_axis=3, tiled=True)
-    columns = lax.all_gather(panels, "chan", axis=2, tiled=True)
-    rows = row_operand(panels)
-    return jnp.einsum(
-        "fqipw,fpjw->fqij", rows, columns, preferred_element_type=jnp.float32
+    groups = lax.axis_size("yhi") * lax.axis_size("core")
+    pairs = lax.axis_size("ylo")
+    bins_local = bin_count // groups
+    weighted = weighted.reshape(groups, bins_local, 2, channels, win_local)
+    outgoing = jnp.broadcast_to(weighted[None], (pairs,) + weighted.shape)
+    outgoing = outgoing.reshape((pairs * groups,) + weighted.shape[1:])
+    incoming = lax.all_to_all(outgoing, ("ylo", "yhi", "core"), 0, 0, tiled=True)
+    incoming = incoming.reshape(pairs, groups, bins_local, 2, channels, win_local)
+    panel = jnp.transpose(incoming, (2, 3, 0, 4, 1, 5)).reshape(
+        bins_local, 2, pairs * channels, groups * win_local
     )
+    own = lax.dynamic_slice_in_dim(panel, lax.axis_index("ylo") * channels, channels, axis=2)
+    rows = row_operand(own)
+
+    split = bins_local // 2
+    first = [jnp.stack(ring_gather(p, "x", 3)) for p in [panel[:split]]][0]
+    second = [jnp.stack(ring_gather(p, "z", 3)) for p in [panel[split:]]][0]
+    first = jnp.stack(ring_gather(first, "z", 4))
+    second = jnp.stack(ring_gather(second, "x", 4))
+    second = jnp.swapaxes(second, 0, 1)
+    gathered = jnp.concatenate([first, second], axis=2)
+    zs, xs = gathered.shape[0], gathered.shape[1]
+    gathered = gathered.reshape(zs, xs, bins_local, 2, pairs, channels, groups * win_local)
+    products = jnp.einsum(
+        "fqipw,ZXfpYcw->fqiZYXc", rows, gathered, preferred_element_type=jnp.float32
+    )
+    z_shift = (zs - lax.axis_index("z")) % zs
+    x_shift = (xs - lax.axis_index("x")) % xs
+    products = jnp.concatenate([products, products], axis=3)
+    products = lax.dynamic_slice_in_dim(products, z_shift, zs, axis=3)
+    products = jnp.concatenate([products, products], axis=5)
+    products = lax.dynamic_slice_in_dim(products, x_shift, xs, axis=5)
+    return products.reshape(bins_local, 2, channels, zs * pairs * xs * channels)
 
 
 def solution(mesh):
+    sizes = dict(zip(mesh.axis_names, mesh.devices.shape))
+    chan, freq = sizes["chan"], sizes["freq"]
+    devices = mesh.devices.reshape(chan // 8, 2, 4, freq // 2, 2)
+    grid = Mesh(devices, ("z", "ylo", "x", "yhi", "core"))
+    chan_axes = ("z", "ylo", "x")
+    freq_axes = ("yhi", "core")
     return jax.shard_map(
         per_device,
-        mesh=mesh,
-        in_specs=(P("chan", "freq", None), P("chan"), P(), P(), P("chan")),
-        out_specs=P("freq", None, "chan", None),
+        mesh=grid,
+        in_specs=(P(chan_axes, freq_axes, None), P(chan_axes), P(), P(), P(chan_axes)),
+        out_specs=P(freq_axes, None, chan_axes, None),
         check_vma=False,
     )

time: 458 us -> 578 us (1.26); the launches traced: 457 us -> 568 us
  waiting for transfers between devices: 362 us -> 208 us
  local copies, waits for them, and re-layouts: 16.4 us -> 146 us
  other arithmetic: 16.2 us -> 121 us
  starting transfers between devices: 0.01 us -> 31.2 us
  between operations: 13.5 us -> 0.49 us
  blocking collectives: 20.4 us -> 31.7 us
    all_gather x1 -> x0, waiting for transfers between devices: 362 us -> none  [per_device(): columns = lax.all_gather(panels, 'chan', axis=2, tiled=True)]
    ppermute x0 -> x16, waiting for transfers between devices: none -> 208 us  [shifted(): lax.ppermute(block, axis, [((i + distance) % size, i) for i in range(size)])]
    concatenate x0 -> x3, other arithmetic: none -> 75.3 us  [the longest x1 27 us: per_device(): products = jnp.concatenate([products, products], axis=3)]
    dynamic_slice x0 -> x1, local copies, waits for them, and re-layouts: none -> 40.9 us  [per_device(): products = lax.dynamic_slice_in_dim(products, x_shift, xs, axis=5)]
    reshape x1 -> x2, local copies, waits for them, and re-layouts: 2.29 us -> 38.5 us  [the longest x1 32.5 us: per_device(): return products.reshape(bins_local, 2, channels, zs * pairs * xs * channels)]
    ppermute x0 -> x16, starting transfers between devices: none -> 31.2 us  [shifted(): lax.ppermute(block, axis, [((i + distance) % size, i) for i in range(size)])]
    slice x0 -> x13, local copies, waits for them, and re-layouts: none -> 29.6 us  [the longest x3 10.6 us: per_device(): first = [jnp.stack(ring_gather(p, 'x', 3)) for p in [panel[:split]]][0]]
    another operation x1 -> x7, other arithmetic: 1.9 us -> 19.9 us  [the longest x2 7.85 us: per_device(): second = jnp.stack(ring_gather(second, 'x', 4))]
  transfers between devices with their start and end apart: 1 -> 16, of which waited for: 1 -> 6; matrix products, arithmetic and copies ran while one was open for 1% -> 13% of each run, Pallas kernels for 0% -> 0%
where the time goes in v2:
time: 578 us; the launch traced here: 568 us
  waiting for transfers between devices  208 us (36%)
  local copies, waits for them, and re-layouts  146 us (25%)
  other arithmetic  121 us (21%)
  blocking collectives  31.7 us (5%)
  starting transfers between devices  31.2 us (5%)
  matrix products  30 us (5%)
    ppermute x16, waiting for transfers between devices, shifted(): lax.ppermute(block, axis, [((i + distance) % size, i) for i in range(size)])  208 us
    dynamic_slice x1, local copies, waits for them, and re-layouts, per_device(): products = lax.dynamic_slice_in_dim(products, x_shift, xs, axis=5)  40.9 us
    reshape x1, local copies, waits for them, and re-layouts, per_device(): return products.reshape(bins_local, 2, channels, zs * pairs * xs * channels)  32.5 us
    all_to_all x1, blocking collectives, per_device(): lax.all_to_all(outgoing, ('ylo', 'yhi', 'core'), 0, 0, tiled=True)  31.7 us
    ppermute x16, starting transfers between devices, shifted(): lax.ppermute(block, axis, [((i + distance) % size, i) for i in range(size)])  31.2 us
    concatenate x1, other arithmetic, per_device(): products = jnp.concatenate([products, products], axis=3)  27 us
    concatenate x1, other arithmetic, per_device(): products = jnp.concatenate([products, products], axis=5)  27 us
    dot_general x1, matrix products, per_device(): jnp.einsum('fqipw,ZXfpYcw->fqiZYXc', rows, gathered, preferred_element_ty...  23.7 us
  transfers between devices with their start and end apart: 16, of which 6 were waited for; matrix products, arithmetic and copies ran while one was open for 13% of the time, Pallas kernels for 0%

profile of v2, /device:TPU:0, one launch (start us, length us, event | category | flops | bytes accessed | tf_op | source)
XLA Modules:
  0.0 567.6 jit_solution(12496832839113938895)
XLA Ops:
  2.3 1.9 multiply_convert_fusion.1
  4.6 10.8 %minimum_convert_fusion = bf16[64,64,1024]{2,1,0:T(8,128)(2,1)} fusion(bf16[64,64,1024]{2,1,0:T(8,128)(2,1)} %param.5, bf16[64]{0:T(256)(128)(2,1)S(1)} %get-tuple-element.16, bf16[64]{0:T(256)(128)(2,1)S(1)} %get-tuple-element.15), kind=kLoop, calls=%fused_computation.10 | loop fusion | flops 25165824 | bytes 16777472 | tf_op jit(solution)/shard_map/convert_element_type | solution.py:54
  15.4 6.3 %fusion.7 = bf16[128,4096]{1,0:T(8,128)(2,1)S(1)} fusion(bf16[1024,128]{0,1:T(8,128)(2,1)S(1)} %convert_element_type.50, bf16[4096,1024]{1,0:T(8,128)(2,1)} %bitcast.66, f32[4096]{0:T(1024)S(1)} %select_n.55), kind=kOutput, calls=%fused_computation.13 | convolution fusion | flops 1074790400 | bytes 9715712 | tf_op jit(solution)/shard_map/dot_general | solution.py:57
  21.7 2.3 broadcast_in_dim.46
  24.0 3.1 broadcast_in_dim.47
  27.1 6.4 %reshape.243 = bf16[8,2,65536]{2,1,0:T(2,128)(2,1)S(1)} reshape(bf16[8,16,2,64,64]{4,3,2,1,0:T(8,128)(2,1)} %bitcast.67) | data formatting | bytes 4194304
  33.4 31.7 %all_to_all.5 = bf16[8,2,65536]{2,1,0:T(2,128)(2,1)} all-to-all(bf16[8,2,65536]{2,1,0:T(2,128)(2,1)S(1)} %reshape.243), channel_id=1, replica_groups=mesh['z'=4,'ylo'=2,'x'=4,'yhi'=2,'core'=2] {'ylo','yhi','core'}, dimensions={0} | all-to-all | bytes 4194304 | tf_op jit(solution)/shard_map/all_to_all | solution.py:73
  65.1 7.4 %reshape.244 = bf16[8,16,2,64,64]{4,3,2,1,0:T(8,128)(2,1)} reshape(bf16[8,2,65536]{2,1,0:T(2,128)(2,1)} %all_to_all.5) | data formatting | bytes 4194304
  72.5 4.9 fusion.22
  77.4 2.0 copy.42
  80.7 2.0 collective-permute-start.10
  82.7 2.2 collective-permute-start.8
  84.9 23.0 %collective-permute-done.10 = bf16[8,2,128,256]{3,2,1,0:T(8,128)(2,1)S(1)} collective-permute-done((bf16[8,2,128,256]{3,2,1,0:T(8,128)(2,1)S(1)}, bf16[8,2,128,256]{3,2,1,0:T(8,128)(2,1)S(1)}, u32[]{:S(2)}, u32[]{:S(2)}) %collective-permute-start.10) | collective-permute-done | bytes 1048608 | tf_op jit(solution)/shard_map/ppermute | solution.py:37
  109.9 3.2 collective-permute-start.9
  113.2 3.6 copy.40
  116.7 2.2 slice.43
  120.4 1.7 collective-permute-start
  122.1 3.5 stack.93
  127.0 4.8 fusion.19
  131.8 1.5 collective-permute-start.12
  133.8 12.7 %collective-permute-done.2 = bf16[8,2,128,256]{3,2,1,0:T(8,128)(2,1)} collective-permute-done((bf16[8,2,128,256]{3,2,1,0:T(8,128)(2,1)}, bf16[8,2,128,256]{3,2,1,0:T(8,128)(2,1)}, u32[]{:S(2)}, u32[]{:S(2)}) %collective-permute-start.2) | collective-permute-done | bytes 1048608 | tf_op jit(solution)/shard_map/ppermute | solution.py:37
  146.5 1.9 slice.58
  148.7 1.9 slice.57
  150.6 2.9 collective-permute-start.1
  154.9 90.3 %collective-permute-done.3 = bf16[8,2,128,128]{3,2,1,0:T(8,128)(2,1)} collective-permute-done((bf16[8,2,128,128]{3,2,1,0:T(8,128)(2,1)}, bf16[8,2,128,128]{3,2,1,0:T(8,128)(2,1)}, u32[]{:S(2)}, u32[]{:S(2)}) %collective-permute-start.3) | collective-permute-done | bytes 524320 | tf_op jit(solution)/shard_map/ppermute | solution.py:37
  246.6 4.8 fusion.20
  251.8 1.6 collective-permute-start.6
  253.4 3.2 slice.64
  256.6 2.9 collective-permute-start.13
  259.5 3.2 slice.65
  262.7 7.9 %collective-permute-start.15 = (bf16[4,8,2,128,128]{4,3,2,1,0:T(8,128)(2,1)}, bf16[4,8,2,128,128]{4,3,2,1,0:T(8,128)(2,1)}, u32[]{:S(2)}, u32[]{:S(2)}) collective-permute-start(bf16[4,8,2,128,128]{4,3,2,1,0:T(8,128)(2,1)} %slice.65), channel_id=1, source_target_pairs={{12,0},{0,4},{4,8},{8,12},{13,1},{1,5},{5,9},{9,13},{14,2},{2,6},{... | collective-permute-start | bytes 6291464 | tf_op jit(solution)/shard_map/ppermute | solution.py:37
  270.7 12.4 %copy.47 = bf16[16,2,2,64,4,64]{5,4,3,2,0,1:T(4,128)(2,1)} copy(bf16[16,2,2,64,4,64]{5,3,1,0,4,2:T(8,128)(2,1)} %bitcast.64) | data formatting | bytes 4194304 | tf_op jit(solution)/shard_map/transpose | solution.py:75
  283.1 6.0 %reshape.238 = bf16[16,2,128,256]{3,2,0,1:T(8,128)(2,1)S(1)} reshape(bf16[16,2,2,64,4,64]{5,4,3,2,0,1:T(4,128)(2,1)} %copy.47) | data formatting | bytes 4194304 | tf_op jit(solution)/shard_map/reshape | solution.py:75
  289.1 52.7 %collective-permute-done.4 = bf16[4,8,2,128,256]{4,3,2,1,0:T(8,128)(2,1)} collective-permute-done((bf16[4,8,2,128,256]{4,3,2,1,0:T(8,128)(2,1)}, bf16[4,8,2,128,256]{4,3,2,1,0:T(8,128)(2,1)}, u32[]{:S(2)}, u32[]{:S(2)}) %collective-permute-start.4) | collective-permute-done | bytes 4194336 | tf_op jit(solution)/shard_map/ppermute | solution.py:37
  341.9 1.7 slice.59
  343.6 1.6 collective-permute-start.5
  345.2 1.7 slice.60
  349.5 3.1 maximum_bitcast_fusion.2
  352.9 10.7 %maximum_bitcast_fusion = bf16[4,4,8,2,128,256]{5,4,3,2,1,0:T(8,128)(2,1)} fusion(bf16[1,4,8,2,128,256]{5,4,3,2,0,1:T(8,128)(2,1)} %bitcast.21, bf16[1,4,8,2,128,256]{5,4,3,2,0,1:T(8,128)(2,1)S(1)} %maximum_bitcast_fusion.2, bf16[1,4,8,2,128,256]{5,4,3,2,0,1:T(8,128)(2,1)} %bitcast.18, bf16[1,4,8,2,128,256]{5,4,3,2,0,1:T(8,128)(2,1)S(1)} %copy-done.2), kind=kLoop, calls=%fused_computation.9 | loop fusion | flops 25165824 | bytes 33554432 | tf_op jit(solution)/shard_map/transpose | solution.py:86
  363.6 24.4 %collective-permute-done.5 = bf16[4,8,2,128,128]{4,3,2,1,0:T(8,128)(2,1)S(1)} collective-permute-done((bf16[4,8,2,128,128]{4,3,2,1,0:T(8,128)(2,1)S(1)}, bf16[4,8,2,128,128]{4,3,2,1,0:T(8,128)(2,1)S(1)}, u32[]{:S(2)}, u32[]{:S(2)}) %collective-permute-start.5) | collective-permute-done | bytes 2097184 | tf_op jit(solution)/shard_map/ppermute | solution.py:37
  387.9 4.4 collective-permute-done.7
  392.3 2.6 maximum_bitcast_fusion.1
  394.9 21.2 %pad_maximum_fusion = bf16[4,4,16,2,128,256]{5,4,3,2,1,0:T(8,128)(2,1)} fusion(bf16[4,4,8,2,128,256]{5,4,3,2,1,0:T(8,128)(2,1)} %maximum_bitcast_fusion, bf16[1,4,8,2,128,256]{5,4,3,2,1,0:T(8,128)(2,1)} %bitcast.10, bf16[1,4,8,2,128,256]{5,4,3,2,1,0:T(8,128)(2,1)} %maximum_bitcast_fusion.1, bf16[1,4,8,2,128,256]{5,4,3,2,1,0:T(8,128)(2,1)} %bitcast.8, ...), kind=kLoop, calls=%fused_computation.6 | loop fusion | flops 67108864 | bytes 67108864 | tf_op jit(solution)/shard_map/concatenate | solution.py:87
  416.2 23.7 %fusion.4 = f32[16,2,64,4,2,4,64]{2,6,1,4,5,3,0:T(8,128)} fusion(bf16[4,4,16,2,2,64,256,1]{6,5,4,3,2,1,0,7:T(8,128)(2,1)} %bitcast.65, bf16[16,1,64,2,256]{4,2,3,1,0:T(8,128)(2,1)} %get-tuple-element.14, bf16[16,1,64,2,256]{4,2,3,1,0:T(8,128)(2,1)} %get-tuple-element.13), kind=kOutput, calls=%fused_computation.11 | convolution fusion | flops 4299161600 | bytes 52428800 | tf_op jit(solution)/shard_map/fqipw,ZXfpYcw->fqiZYXc/dot_general | solution.py:90
  439.9 27.0 %fusion.1 = f32[16,2,64,4,2,4,64]{2,6,1,4,5,3,0:T(8,128)} fusion(s32[]{:T(128)S(6)} %select_n.58, f32[16,2,64,4,2,4,64]{2,6,1,4,5,3,0:T(8,128)} %fusion.4), kind=kLoop, calls=%fused_computation.5 | loop fusion | flops 4194304 | bytes 33554436 | tf_op jit(solution)/shard_map/concatenate | solution.py:95
  466.9 27.0 %fusion = f32[16,2,64,4,2,4,64]{2,6,1,4,5,3,0:T(8,128)} fusion(s32[]{:T(128)S(6)} %select_n.60, f32[16,2,64,4,2,4,64]{2,6,1,4,5,3,0:T(8,128)} %fusion.1), kind=kLoop, calls=%fused_computation.4 | loop fusion | flops 4194304 | bytes 33554436 | tf_op jit(solution)/shard_map/concatenate | solution.py:97
  493.9 40.9 %copy.50 = f32[16,2,64,4,2,4,64]{6,5,4,3,2,1,0:T(4,128)} copy(f32[16,2,64,4,2,4,64]{2,6,1,4,5,3,0:T(8,128)} %fusion) | data formatting | bytes 33554432 | tf_op jit(solution)/shard_map/dynamic_slice | solution.py:98
  534.9 32.5 %reshape.239 = f32[16,2,64,2048]{3,2,1,0:T(8,128)} reshape(f32[16,2,64,4,2,4,64]{6,5,4,3,2,1,0:T(4,128)} %copy.50) | data formatting | bytes 33554432 | tf_op jit(solution)/shard_map/reshape | solution.py:99
  (45 shorter events, 15.7 us)
Async XLA Ops:
  79.3 33.8 %copy-start = (bf16[8,2,2,64,4,64]{5,4,3,2,1,0:T(4,128)(2,1)}, bf16[8,2,2,64,4,64]{5,4,3,2,1,0:T(4,128)(2,1)S(1)}, u32[]{:S(2)}) copy-start(bf16[8,2,2,64,4,64]{5,4,3,2,1,0:T(4,128)(2,1)S(1)} %copy.42) | copy-start | bytes 3145732
  80.7 27.2 %collective-permute-start.10 = (bf16[8,2,128,256]{3,2,1,0:T(8,128)(2,1)S(1)}, bf16[8,2,128,256]{3,2,1,0:T(8,128)(2,1)S(1)}, u32[]{:S(2)}, u32[]{:S(2)}) collective-permute-start(bf16[8,2,128,256]{3,2,1,0:T(8,128)(2,1)S(1)} %slice.49), channel_id=1, source_target_pairs={{96,0},{0,32},{32,64},{64,96},{97,1},{1,33},{33,65},{65,97},{98,2}... | collective-permute-start | bytes 3145736 | tf_op jit(solution)/shard_map/ppermute | solution.py:37
  82.7 26.2 %collective-permute-start.8 = (bf16[8,2,128,256]{3,2,1,0:T(8,128)(2,1)S(1)}, bf16[8,2,128,256]{3,2,1,0:T(8,128)(2,1)S(1)}, u32[]{:S(2)}, u32[]{:S(2)}) collective-permute-start(bf16[8,2,128,256]{3,2,1,0:T(8,128)(2,1)S(1)} %slice.49), channel_id=1, source_target_pairs={{32,0},{64,32},{96,64},{0,96},{33,1},{65,33},{97,65},{1,97},{34,2}... | collective-permute-start | bytes 3145736 | tf_op jit(solution)/shard_map/ppermute | solution.py:37
  107.9 5.3 copy-start.3
  108.9 16.7 %collective-permute-start.11 = (bf16[8,2,128,128]{3,2,1,0:T(8,128)(2,1)}, bf16[8,2,128,128]{3,2,1,0:T(8,128)(2,1)}, u32[]{:S(2)}, u32[]{:S(2)}) collective-permute-start(bf16[8,2,128,128]{3,2,1,0:T(8,128)(2,1)} %slice.63), channel_id=1, source_target_pairs={{96,0},{0,32},{32,64},{64,96},{97,1},{1,33},{33,65},{65,97},{98,2}... | collective-permute-start | bytes 1572872 | tf_op jit(solution)/shard_map/ppermute | solution.py:37
  108.9 4.3 copy-start.4
  109.9 15.7 %collective-permute-start.9 = (bf16[8,2,128,128]{3,2,1,0:T(8,128)(2,1)}, bf16[8,2,128,128]{3,2,1,0:T(8,128)(2,1)}, u32[]{:S(2)}, u32[]{:S(2)}) collective-permute-start(bf16[8,2,128,128]{3,2,1,0:T(8,128)(2,1)} %slice.62), channel_id=1, source_target_pairs={{32,0},{64,32},{96,64},{0,96},{33,1},{65,33},{97,65},{1,97},{34,2}... | collective-permute-start | bytes 1572872 | tf_op jit(solution)/shard_map/ppermute | solution.py:37
  118.9 27.6 %collective-permute-start.2 = (bf16[8,2,128,256]{3,2,1,0:T(8,128)(2,1)}, bf16[8,2,128,256]{3,2,1,0:T(8,128)(2,1)}, u32[]{:S(2)}, u32[]{:S(2)}) collective-permute-start(bf16[8,2,128,256]{3,2,1,0:T(8,128)(2,1)} %slice.43), channel_id=1, source_target_pairs={{12,0},{0,4},{4,8},{8,12},{13,1},{1,5},{5,9},{9,13},{14,2},{2,6},{... | collective-permute-start | bytes 3145736 | tf_op jit(solution)/shard_map/ppermute | solution.py:37
  120.4 28.3 %collective-permute-start = (bf16[8,2,128,256]{3,2,1,0:T(8,128)(2,1)}, bf16[8,2,128,256]{3,2,1,0:T(8,128)(2,1)}, u32[]{:S(2)}, u32[]{:S(2)}) collective-permute-start(bf16[8,2,128,256]{3,2,1,0:T(8,128)(2,1)} %slice.43), channel_id=1, source_target_pairs={{4,0},{8,4},{12,8},{0,12},{5,1},{9,5},{13,9},{1,13},{6,2},{10,6},{... | collective-permute-start | bytes 3145736 | tf_op jit(solution)/shard_map/ppermute | solution.py:37
  131.8 121.7 %collective-permute-start.12 = (bf16[4,8,2,128,256]{4,3,2,1,0:T(8,128)(2,1)}, bf16[4,8,2,128,256]{4,3,2,1,0:T(8,128)(2,1)}, u32[]{:S(2)}, u32[]{:S(2)}) collective-permute-start(bf16[4,8,2,128,256]{4,3,2,1,0:T(8,128)(2,1)} %get-tuple-element.12), channel_id=1, source_target_pairs={{4,0},{8,4},{12,8},{0,12},{5,1},{9,5},{13,9},{1,13},{6,2},{10,6},{... | collective-permute-start | bytes 12582920 | tf_op jit(solution)/shard_map/ppermute | solution.py:37
  133.3 126.2 %collective-permute-start.14 = (bf16[4,8,2,128,256]{4,3,2,1,0:T(8,128)(2,1)}, bf16[4,8,2,128,256]{4,3,2,1,0:T(8,128)(2,1)}, u32[]{:S(2)}, u32[]{:S(2)}) collective-permute-start(bf16[4,8,2,128,256]{4,3,2,1,0:T(8,128)(2,1)} %get-tuple-element.12), channel_id=1, source_target_pairs={{12,0},{0,4},{4,8},{8,12},{13,1},{1,5},{5,9},{9,13},{14,2},{2,6},{... | collective-permute-start | bytes 12582920 | tf_op jit(solution)/shard_map/ppermute | solution.py:37
  148.4 96.8 %collective-permute-start.3 = (bf16[8,2,128,128]{3,2,1,0:T(8,128)(2,1)}, bf16[8,2,128,128]{3,2,1,0:T(8,128)(2,1)}, u32[]{:S(2)}, u32[]{:S(2)}) collective-permute-start(bf16[8,2,128,128]{3,2,1,0:T(8,128)(2,1)} %slice.58), channel_id=1, source_target_pairs={{12,0},{0,4},{4,8},{8,12},{13,1},{1,5},{5,9},{9,13},{14,2},{2,6},{... | collective-permute-start | bytes 1572872 | tf_op jit(solution)/shard_map/ppermute | solution.py:37
  150.6 94.6 %collective-permute-start.1 = (bf16[8,2,128,128]{3,2,1,0:T(8,128)(2,1)}, bf16[8,2,128,128]{3,2,1,0:T(8,128)(2,1)}, u32[]{:S(2)}, u32[]{:S(2)}) collective-permute-start(bf16[8,2,128,128]{3,2,1,0:T(8,128)(2,1)} %slice.57), channel_id=1, source_target_pairs={{4,0},{8,4},{12,8},{0,12},{5,1},{9,5},{13,9},{1,13},{6,2},{10,6},{... | collective-permute-start | bytes 1572872 | tf_op jit(solution)/shard_map/ppermute | solution.py:37
  251.4 90.5 %collective-permute-start.4 = (bf16[4,8,2,128,256]{4,3,2,1,0:T(8,128)(2,1)}, bf16[4,8,2,128,256]{4,3,2,1,0:T(8,128)(2,1)}, u32[]{:S(2)}, u32[]{:S(2)}) collective-permute-start(bf16[4,8,2,128,256]{4,3,2,1,0:T(8,128)(2,1)} %get-tuple-element.8), channel_id=1, source_target_pairs={{32,0},{64,32},{96,64},{0,96},{33,1},{65,33},{97,65},{1,97},{34,2}... | collective-permute-start | bytes 12582920 | tf_op jit(solution)/shard_map/ppermute | solution.py:37
  251.8 93.4 %collective-permute-start.6 = (bf16[4,8,2,128,256]{4,3,2,1,0:T(8,128)(2,1)}, bf16[4,8,2,128,256]{4,3,2,1,0:T(8,128)(2,1)}, u32[]{:S(2)}, u32[]{:S(2)}) collective-permute-start(bf16[4,8,2,128,256]{4,3,2,1,0:T(8,128)(2,1)} %get-tuple-element.8), channel_id=1, source_target_pairs={{96,0},{0,32},{32,64},{64,96},{97,1},{1,33},{33,65},{65,97},{98,2}... | collective-permute-start | bytes 12582920 | tf_op jit(solution)/shard_map/ppermute | solution.py:37
  256.6 92.9 %collective-permute-start.13 = (bf16[4,8,2,128,128]{4,3,2,1,0:T(8,128)(2,1)}, bf16[4,8,2,128,128]{4,3,2,1,0:T(8,128)(2,1)}, u32[]{:S(2)}, u32[]{:S(2)}) collective-permute-start(bf16[4,8,2,128,128]{4,3,2,1,0:T(8,128)(2,1)} %slice.64), channel_id=1, source_target_pairs={{4,0},{8,4},{12,8},{0,12},{5,1},{9,5},{13,9},{1,13},{6,2},{10,6},{... | collective-permute-start | bytes 6291464 | tf_op jit(solution)/shard_map/ppermute | solution.py:37
  262.7 86.7 %collective-permute-start.15 = (bf16[4,8,2,128,128]{4,3,2,1,0:T(8,128)(2,1)}, bf16[4,8,2,128,128]{4,3,2,1,0:T(8,128)(2,1)}, u32[]{:S(2)}, u32[]{:S(2)}) collective-permute-start(bf16[4,8,2,128,128]{4,3,2,1,0:T(8,128)(2,1)} %slice.65), channel_id=1, source_target_pairs={{12,0},{0,4},{4,8},{8,12},{13,1},{1,5},{5,9},{9,13},{14,2},{2,6},{... | collective-permute-start | bytes 6291464 | tf_op jit(solution)/shard_map/ppermute | solution.py:37
  343.6 44.4 %collective-permute-start.5 = (bf16[4,8,2,128,128]{4,3,2,1,0:T(8,128)(2,1)S(1)}, bf16[4,8,2,128,128]{4,3,2,1,0:T(8,128)(2,1)S(1)}, u32[]{:S(2)}, u32[]{:S(2)}) collective-permute-start(bf16[4,8,2,128,128]{4,3,2,1,0:T(8,128)(2,1)S(1)} %slice.59), channel_id=1, source_target_pairs={{32,0},{64,32},{96,64},{0,96},{33,1},{65,33},{97,65},{1,97},{34,2}... | collective-permute-start | bytes 6291464 | tf_op jit(solution)/shard_map/ppermute | solution.py:37
  346.9 45.4 %collective-permute-start.7 = (bf16[4,8,2,128,128]{4,3,2,1,0:T(8,128)(2,1)S(1)}, bf16[4,8,2,128,128]{4,3,2,1,0:T(8,128)(2,1)S(1)}, u32[]{:S(2)}, u32[]{:S(2)}) collective-permute-start(bf16[4,8,2,128,128]{4,3,2,1,0:T(8,128)(2,1)S(1)} %slice.60), channel_id=1, source_target_pairs={{96,0},{0,32},{32,64},{64,96},{97,1},{1,33},{33,65},{65,97},{98,2}... | collective-permute-start | bytes 6291464 | tf_op jit(solution)/shard_map/ppermute | solution.py:37
  349.4 3.4 copy-start.2
  363.5 31.4 %copy-start.1 = (bf16[1,4,8,2,128,256]{5,4,3,2,1,0:T(8,128)(2,1)S(1)}, bf16[1,4,8,2,128,256]{5,4,3,2,1,0:T(8,128)(2,1)}, u32[]{:S(2)}) copy-start(bf16[1,4,8,2,128,256]{5,4,3,2,1,0:T(8,128)(2,1)} %get-tuple-element.7) | copy-start | bytes 12582916
